TPU v7x, 256 devices: a whole 4x4x8 slice. The times are simulated.
256 devices in a mesh: group: 4 (over y), key: 64 (over z, x, core).
Axes of the slice: x: 4, y: 4, z: 8, core: 2. Of those that a mesh axis runs over, the one named last changes fastest.
Arguments:
- src_desc: bfloat16 [65536, 256], P(('group', 'key'))
- tgt_desc: bfloat16 [131072, 256], P('key')
- src_weight: float32 [65536], P(('group', 'key')), may hold values from 0.05 to 20
- tgt_weight: float32 [131072], P('key'), may hold values from 0.05 to 20
- tgt_dual: float32 [131072], P('key'), may hold values from -1.2 to 1.2
- pair_blocks: int32 [4, 64, 2, 64], P('group', 'key'), may hold values from 0 to 63, as said below
- pair_count: int32 [4, 64], P('group', 'key'), may hold values from 8 to 64, as said below
Outputs:
- src_dual: float32 [65536], P(('group', 'key'))
- tgt_dual_new: float32 [131072], P('key')
Inputs may be any that keep to these rules, and one draw needn't show every extreme that they name: `pair_blocks`: row 0 holds source clusters 0 to 63, row 1 target clusters 0 to 7; the live slots of one device are distinct pairs; every source cluster and every target cluster is in some live pair. `pair_count`: live slots come first.
All inputs are finite; a program needn't handle non-finite values.
Results may differ from a plain program's by a relative error of at most 0.0003.
Values may be sent and summed in bfloat16 or wider, within the bound.
No kernel may reach another device: no remote copies, remote signals or barrier semaphores. Data moves between devices by JAX's collectives and lax.ppermute only.
A program may use at most 64 MiB of HBM per device.

v0:
```python
import functools

import jax
import jax.numpy as jnp
from jax import lax
from jax.experimental import pallas as pl
from jax.experimental.pallas import tpu as pltpu
from jax.sharding import PartitionSpec as P

CLUSTER = 256
UNROLL = 4

ENTROPY = 0.05
INV_ENTROPY = 20.0
NEG_FLOOR = -1e30


def _slot_ids(ids_ref, slot, src_clusters, tgt_clusters):
    src_id = jnp.minimum(jnp.maximum(ids_ref[0, slot], 0), src_clusters - 1)
    tgt_id = jnp.minimum(jnp.maximum(ids_ref[1, slot], 0), tgt_clusters - 1)
    return src_id, tgt_id


def _block_cost(src_ref, tgt_ref, sqs_ref, sqt_ref, src_id, tgt_id, width):
    src_start = pl.multiple_of(src_id * CLUSTER, CLUSTER)
    tgt_start = pl.multiple_of(tgt_id * CLUSTER, CLUSTER)
    src_rows = src_ref[pl.ds(src_start, CLUSTER), :]
    tgt_rows = tgt_ref[pl.ds(tgt_start, CLUSTER), :]
    inner = lax.dot_general(
        tgt_rows, src_rows, (((1,), (1,)), ((), ())), preferred_element_type=jnp.float32
    )
    sq_s = sqs_ref[pl.ds(src_id, 1), :]
    sq_t = sqt_ref[pl.ds(tgt_start, CLUSTER), :]
    return (sq_s + sq_t) - (2.0 / width) * inner


def _first_kernel(ids_ref, cnt_ref, src_ref, tgt_ref, sqs_ref, sqt_ref, pot_ref, top_ref, tot_ref):
    src_clusters = sqs_ref.shape[0]
    tgt_clusters = tgt_ref.shape[0] // CLUSTER
    width = src_ref.shape[1]
    top_ref[...] = jnp.full(top_ref.shape, NEG_FLOOR, jnp.float32)
    tot_ref[...] = jnp.zeros(tot_ref.shape, jnp.float32)
    count = jnp.minimum(jnp.maximum(cnt_ref[0], 0), ids_ref.shape[1])

    def scores_of(slot):
        src_id, tgt_id = _slot_ids(ids_ref, slot, src_clusters, tgt_clusters)
        cost = _block_cost(src_ref, tgt_ref, sqs_ref, sqt_ref, src_id, tgt_id, width)
        pot = pot_ref[pl.ds(pl.multiple_of(tgt_id * CLUSTER, CLUSTER), CLUSTER), :]
        return src_id, (pot - cost) * INV_ENTROPY

    def update(src_id, scores):
        peak = jnp.max(scores, axis=0, keepdims=True)
        old_top = top_ref[pl.ds(src_id, 1), :]
        old_tot = tot_ref[pl.ds(src_id, 1), :]
        new_top = jnp.maximum(old_top, peak)
        new_tot = old_tot * jnp.exp(old_top - new_top) + jnp.sum(
            jnp.exp(scores - new_top), axis=0, keepdims=True
        )
        top_ref[pl.ds(src_id, 1), :] = new_top
        tot_ref[pl.ds(src_id, 1), :] = new_tot

    def body(trip, carry):
        blocks = [scores_of(UNROLL * trip + lane) for lane in range(UNROLL)]
        for block in blocks:
            update(*block)
        return carry

    def tail(slot, carry):
        update(*scores_of(slot))
        return carry

    lax.fori_loop(0, count // UNROLL, body, 0)
    lax.fori_loop(count // UNROLL * UNROLL, count, tail, 0)


def _second_kernel(ids_ref, cnt_ref, src_ref, tgt_ref, sqs_ref, sqt_ref, dual_ref, top_ref, tot_ref):
    src_clusters = sqs_ref.shape[0]
    tgt_clusters = tgt_ref.shape[0] // CLUSTER
    width = src_ref.shape[1]
    top_ref[...] = jnp.full(top_ref.shape, NEG_FLOOR, jnp.float32)
    tot_ref[...] = jnp.zeros(tot_ref.shape, jnp.float32)
    count = jnp.minimum(jnp.maximum(cnt_ref[0], 0), ids_ref.shape[1])

    def scores_of(slot):
        src_id, tgt_id = _slot_ids(ids_ref, slot, src_clusters, tgt_clusters)
        cost = _block_cost(src_ref, tgt_ref, sqs_ref, sqt_ref, src_id, tgt_id, width)
        pot = dual_ref[pl.ds(src_id, 1), :]
        return tgt_id, (pot - cost) * INV_ENTROPY

    def update(tgt_id, scores):
        peak = jnp.max(scores, axis=1, keepdims=True)
        tgt_rows = pl.ds(pl.multiple_of(tgt_id * CLUSTER, CLUSTER), CLUSTER)
        old_top = top_ref[tgt_rows, :]
        old_tot = tot_ref[tgt_rows, :]
        new_top = jnp.maximum(old_top, peak)
        new_tot = old_tot * jnp.exp(old_top - new_top) + jnp.sum(
            jnp.exp(scores - new_top), axis=1, keepdims=True
        )
        top_ref[tgt_rows, :] = new_top
        tot_ref[tgt_rows, :] = new_tot

    def body(trip, carry):
        blocks = [scores_of(UNROLL * trip + lane) for lane in range(UNROLL)]
        for block in blocks:
            update(*block)
        return carry

    def tail(slot, carry):
        update(*scores_of(slot))
        return carry

    lax.fori_loop(0, count // UNROLL, body, 0)
    lax.fori_loop(count // UNROLL * UNROLL, count, tail, 0)


def _sweep(kernel, out_shape, ids, cnt, group_src, tgt_desc, sq_src, sq_tgt, pot):
    vmem = pl.BlockSpec(memory_space=pltpu.VMEM)
    smem = pl.BlockSpec(memory_space=pltpu.SMEM)
    slots = ids.shape[1]
    flops = 2 * slots * CLUSTER * CLUSTER * group_src.shape[1]
    return pl.pallas_call(
        kernel,
        out_shape=(out_shape, out_shape),
        in_specs=[smem, smem, vmem, vmem, vmem, vmem, vmem],
        out_specs=(vmem, vmem),
        compiler_params=pltpu.CompilerParams(vmem_limit_bytes=48 * 1024 * 1024),
        cost_estimate=pl.CostEstimate(
            flops=flops,
            transcendentals=slots * CLUSTER * CLUSTER,
            bytes_accessed=group_src.size * 2 + tgt_desc.size * 2,
        ),
    )(ids, cnt, group_src, tgt_desc, sq_src, sq_tgt, pot)


def merge_lse(first, second):
    top = jnp.maximum(first, second)
    return top + jnp.log1p(jnp.exp(jnp.minimum(first, second) - top))


def butterfly(lse, weight, axis, size, index):
    bit = 1
    rows = lse.shape[0]
    while bit < size:
        perm = [(i, i ^ bit) for i in range(size)]
        other = lax.ppermute(jnp.concatenate([lse, weight], axis=0), axis, perm)
        lse = merge_lse(lse, other[:rows])
        is_low = (index & bit) == 0
        low = jnp.where(is_low, weight, other[rows:])
        high = jnp.where(is_low, other[rows:], weight)
        weight = jnp.concatenate([low, high], axis=0)
        bit *= 2
    return lse, weight


def local(src_desc, tgt_desc, src_weight, tgt_weight, tgt_dual, pair_blocks, pair_count):
    width = src_desc.shape[1]
    own_clusters = src_desc.shape[0] // CLUSTER
    key_size = lax.axis_size("key")
    src_clusters = own_clusters * key_size
    tgt_clusters = tgt_desc.shape[0] // CLUSTER
    slot_total = pair_blocks.shape[3]
    ids = pair_blocks.reshape(2, slot_total)
    cnt = pair_count.reshape(1)

    group_src = lax.all_gather(src_desc, "key", axis=0, tiled=True)
    sq_src = (jnp.sum(group_src.astype(jnp.float32) ** 2, axis=1) / width).reshape(src_clusters, CLUSTER)

    sq_tgt = (jnp.sum(tgt_desc.astype(jnp.float32) ** 2, axis=1) / width).reshape(-1, 1)
    pot_col = tgt_dual.reshape(-1, 1)

    src_shape = jax.ShapeDtypeStruct((src_clusters, CLUSTER), jnp.float32)
    src_tops, src_totals = _sweep(
        _first_kernel, src_shape, ids, cnt, group_src, tgt_desc, sq_src, sq_tgt, pot_col
    )
    key_index = lax.axis_index("key")
    local_lse = jnp.maximum(src_tops + jnp.log(src_totals), NEG_FLOOR)
    group_lse, group_weight = butterfly(
        local_lse, src_weight.reshape(own_clusters, CLUSTER), "key", key_size, key_index
    )
    group_dual = ENTROPY * jnp.log(group_weight) - ENTROPY * group_lse
    share_start = key_index * own_clusters
    src_dual = lax.dynamic_slice_in_dim(group_dual, share_start, own_clusters, 0).reshape(-1)

    tgt_shape = jax.ShapeDtypeStruct((tgt_clusters * CLUSTER, 1), jnp.float32)
    tgt_tops, tgt_totals = _sweep(
        _second_kernel, tgt_shape, ids, cnt, group_src, tgt_desc, sq_src, sq_tgt, group_dual
    )
    tgt_pack = jnp.stack([tgt_tops.reshape(tgt_clusters, CLUSTER), tgt_totals.reshape(tgt_clusters, CLUSTER)])
    all_pack = lax.all_gather(tgt_pack, "group", axis=0)
    tops4 = all_pack[:, 0]
    tots4 = all_pack[:, 1]
    merged_top = jnp.max(tops4, axis=0)
    merged_total = jnp.sum(tots4 * jnp.exp(tops4 - merged_top[None]), axis=0)
    tgt_lse = (merged_top + jnp.log(merged_total)).reshape(-1)
    tgt_dual_new = ENTROPY * jnp.log(tgt_weight) - ENTROPY * tgt_lse
    return (src_dual, tgt_dual_new)


def solution(mesh):
    in_specs = (
        P(("group", "key"), None),
        P("key", None),
        P(("group", "key")),
        P("key"),
        P("key"),
        P("group", "key", None, None),
        P("group", "key"),
    )
    out_specs = (P(("group", "key")), P("key"))
    return jax.shard_map(local, mesh=mesh, in_specs=in_specs, out_specs=out_specs, check_vma=False)
```

profile of v0, /device:TPU:8, one launch (start us, length us, event | category | flops | bytes accessed | tf_op | source)
XLA Modules:
  0.0 187.9 jit_solution(7370176381962904854)
XLA Ops:
  7.2 0.0 copy-start
  7.2 0.0 copy-start.2
  7.2 0.0 all-gather.3.cloned.1.call-start
  7.2 0.7 all-gather.3.cloned.1.call-update
  8.6 1.6 multiply_reduce_fusion.1
  10.2 0.4 copy.14.sqt_ref
  10.5 1.1 copy.15.pot_ref
  11.6 0.0 copy-start.4
  11.6 85.0 %all-gather.3.cloned.1.call-done.src_ref = bf16[16384,256]{1,0:T(8,128)(2,1)} async-done(((bf16[256,256]{1,0:T(8,128)(2,1)}), bf16[16384,256]{1,0:T(8,128)(2,1)}) %all-gather.3.cloned.1.call-update) | async-done | bytes 8388624 | tf_op jit(solution)/shard_map/all_gather | solution.py:165
  96.6 5.2 %multiply_reduce_fusion = f32[16384]{0:T(1024)S(1)} fusion(bf16[16384,256]{1,0:T(8,128)(2,1)} %all-gather.3.cloned.1.call-done.src_ref), kind=kLoop, calls=%fused_computation | loop fusion | flops 12566528 | bytes 8454144 | tf_op jit(solution)/shard_map/reduce_sum | solution.py:166
  101.9 11.6 %shard_map.86 = (f32[64,256]{1,0:T(8,128)S(1)}, f32[64,256]{1,0:T(8,128)S(1)}) custom-call(s32[2,64]{1,0:T(2,128)S(1)} %bitcast.27, s32[1]{0:T(128)} %bitcast.25.cnt_ref, bf16[16384,256]{1,0:T(8,128)(2,1)} %all-gather.3.cloned.1.call-done.src_ref, bf16[2048,256]{1,0:T(8,128)(2,1)S(1)} %copy-done, f32[64,256]{1,0:T(8,128)S(1)} %div.18.sqs_ref, ...), custom_call_target="tpu_custom_call" | custom-call | flops 2147483648 | bytes 9437184 | tf_op jit(solution)/shard_map/pallas_call | solution.py:121
  113.5 0.0 copy-start.3
  113.6 1.9 %collective-permute-start = (f32[65,256]{1,0:T(8,128)S(1)}, f32[65,256]{1,0:T(8,128)S(1)}, u32[]{:S(2)}, u32[]{:S(2)}) collective-permute-start(f32[65,256]{1,0:T(8,128)S(1)} %pad_maximum_fusion.2), channel_id=1, source_target_pairs={{0,1},{1,0},{2,3},{3,2},{4,5},{5,4},{6,7},{7,6},{8,9},{9,8},{10,11... | collective-permute-start | bytes 199688 | tf_op jit(solution)/shard_map/ppermute | solution.py:145
  115.4 0.9 collective-permute-done
  116.4 0.1 collective-permute-start.1
  116.5 4.5 %collective-permute-done.1 = f32[66,256]{1,0:T(8,128)S(1)} collective-permute-done((f32[66,256]{1,0:T(8,128)S(1)}, f32[66,256]{1,0:T(8,128)S(1)}, u32[]{:S(2)}, u32[]{:S(2)}) %collective-permute-start.1) | collective-permute-done | bytes 67616 | tf_op jit(solution)/shard_map/ppermute | solution.py:145
  121.1 0.4 collective-permute-start.2
  121.5 5.6 %collective-permute-done.2 = f32[68,256]{1,0:T(8,128)S(1)} collective-permute-done((f32[68,256]{1,0:T(8,128)S(1)}, f32[68,256]{1,0:T(8,128)S(1)}, u32[]{:S(2)}, u32[]{:S(2)}) %collective-permute-start.2) | collective-permute-done | bytes 69664 | tf_op jit(solution)/shard_map/ppermute | solution.py:145
  127.2 0.1 collective-permute-start.3
  127.3 4.3 %collective-permute-done.3 = f32[72,256]{1,0:T(8,128)S(1)} collective-permute-done((f32[72,256]{1,0:T(8,128)S(1)}, f32[72,256]{1,0:T(8,128)S(1)}, u32[]{:S(2)}, u32[]{:S(2)}) %collective-permute-start.3) | collective-permute-done | bytes 73760 | tf_op jit(solution)/shard_map/ppermute | solution.py:145
  131.7 0.1 collective-permute-start.4
  131.8 6.8 %collective-permute-done.4 = f32[80,256]{1,0:T(8,128)S(1)} collective-permute-done((f32[80,256]{1,0:T(8,128)S(1)}, f32[80,256]{1,0:T(8,128)S(1)}, u32[]{:S(2)}, u32[]{:S(2)}) %collective-permute-start.4) | collective-permute-done | bytes 81952 | tf_op jit(solution)/shard_map/ppermute | solution.py:145
  138.7 0.1 collective-permute-start.5
  138.8 9.3 %collective-permute-done.5 = f32[96,256]{1,0:T(8,128)S(1)} collective-permute-done((f32[96,256]{1,0:T(8,128)S(1)}, f32[96,256]{1,0:T(8,128)S(1)}, u32[]{:S(2)}, u32[]{:S(2)}) %collective-permute-start.5) | collective-permute-done | bytes 98336 | tf_op jit(solution)/shard_map/ppermute | solution.py:145
  148.1 0.1 fusion.1.dual_ref
  148.2 0.6 constant_dynamic-slice_fusion
  148.7 18.1 %shard_map.87 = (f32[2048,1]{1,0:T(8,128)S(1)}, f32[2048,1]{1,0:T(8,128)S(1)}) custom-call(s32[2,64]{1,0:T(2,128)S(1)} %bitcast.28, s32[1]{0:T(128)} %bitcast.26.cnt_ref, bf16[16384,256]{1,0:T(8,128)(2,1)} %all-gather.3.cloned.1.call-done.src_ref, bf16[2048,256]{1,0:T(8,128)(2,1)S(1)} %copy-done, f32[64,256]{1,0:T(8,128)S(1)} %div.18.sqs_ref, ...), custom_call_target="tpu_custom_call" | custom-call | flops 2147483648 | bytes 9437184 | tf_op jit(solution)/shard_map/pallas_call | solution.py:121
  166.8 1.0 copy-done.1
  167.8 1.6 reduce.1
  169.4 0.3 reduce.2
  169.7 10.7 %all-gather = f32[8,8,256]{2,1,0:T(8,128)S(1)} all-gather(f32[2,8,256]{2,1,0:T(8,128)S(1)} %pad_maximum_fusion.8), channel_id=2, replica_groups=mesh['group'=4,'key'=64] {'group'}, dimensions={0}, use_global_device_ids=true | all-gather | bytes 81920 | tf_op jit(solution)/shard_map/all_gather | solution.py:189
  180.5 0.6 multiply_subtract_fusion
  (33 shorter events, 0.5 us)
Async XLA Ops:
  7.2 94.7 %copy-start = (bf16[2048,256]{1,0:T(8,128)(2,1)S(1)}, bf16[2048,256]{1,0:T(8,128)(2,1)}, u32[]{:S(2)}) copy-start(bf16[2048,256]{1,0:T(8,128)(2,1)} %tgt_ref.3) | copy-start | bytes 3145732
  7.2 94.7 %copy-start.2 = (s32[1,1,2,64]{3,2,1,0:T(2,128)S(1)}, s32[1,1,2,64]{3,2,1,0:T(2,128)}, u32[]{:S(2)}) copy-start(s32[1,1,2,64]{3,2,1,0:T(2,128)} %param.12) | copy-start | bytes 1540
  7.2 89.4 %all-gather.3.cloned.1.call-start = ((), (), s32[]{:S(2)}) async-start(), calls=%async_computation | async-start | bytes 8519680 | tf_op jit(solution)/shard_map/all_gather | solution.py:165
  11.6 101.9 %copy-start.4 = (f32[256]{0:T(256)S(1)}, f32[256]{0:T(256)}, u32[]{:S(2)}) copy-start(f32[256]{0:T(256)} %param.9) | copy-start | bytes 3076
  113.5 67.0 %copy-start.3 = (f32[2048]{0:T(1024)S(1)}, f32[2048]{0:T(1024)}, u32[]{:S(2)}) copy-start(f32[2048]{0:T(1024)} %param.10) | copy-start | bytes 24580
  113.6 2.8 %collective-permute-start = (f32[65,256]{1,0:T(8,128)S(1)}, f32[65,256]{1,0:T(8,128)S(1)}, u32[]{:S(2)}, u32[]{:S(2)}) collective-permute-start(f32[65,256]{1,0:T(8,128)S(1)} %pad_maximum_fusion.2), channel_id=1, source_target_pairs={{0,1},{1,0},{2,3},{3,2},{4,5},{5,4},{6,7},{7,6},{8,9},{9,8},{10,11... | collective-permute-start | bytes 199688 | tf_op jit(solution)/shard_map/ppermute | solution.py:145
  116.4 4.6 %collective-permute-start.1 = (f32[66,256]{1,0:T(8,128)S(1)}, f32[66,256]{1,0:T(8,128)S(1)}, u32[]{:S(2)}, u32[]{:S(2)}) collective-permute-start(f32[66,256]{1,0:T(8,128)S(1)} %pad_maximum_fusion.3), channel_id=1, source_target_pairs={{0,2},{1,3},{2,0},{3,1},{4,6},{5,7},{6,4},{7,5},{8,10},{9,11},{10,... | collective-permute-start | bytes 202760 | tf_op jit(solution)/shard_map/ppermute | solution.py:145
  121.1 5.9 %collective-permute-start.2 = (f32[68,256]{1,0:T(8,128)S(1)}, f32[68,256]{1,0:T(8,128)S(1)}, u32[]{:S(2)}, u32[]{:S(2)}) collective-permute-start(f32[68,256]{1,0:T(8,128)S(1)} %pad_maximum_fusion.4), channel_id=1, source_target_pairs={{0,4},{1,5},{2,6},{3,7},{4,0},{5,1},{6,2},{7,3},{8,12},{9,13},{10,... | collective-permute-start | bytes 208904 | tf_op jit(solution)/shard_map/ppermute | solution.py:145
  127.2 4.4 %collective-permute-start.3 = (f32[72,256]{1,0:T(8,128)S(1)}, f32[72,256]{1,0:T(8,128)S(1)}, u32[]{:S(2)}, u32[]{:S(2)}) collective-permute-start(f32[72,256]{1,0:T(8,128)S(1)} %pad_maximum_fusion.5), channel_id=1, source_target_pairs={{0,8},{1,9},{2,10},{3,11},{4,12},{5,13},{6,14},{7,15},{8,0},{9,1},... | collective-permute-start | bytes 221192 | tf_op jit(solution)/shard_map/ppermute | solution.py:145
  131.7 6.9 %collective-permute-start.4 = (f32[80,256]{1,0:T(8,128)S(1)}, f32[80,256]{1,0:T(8,128)S(1)}, u32[]{:S(2)}, u32[]{:S(2)}) collective-permute-start(f32[80,256]{1,0:T(8,128)S(1)} %pad_maximum_fusion.1), channel_id=1, source_target_pairs={{0,16},{1,17},{2,18},{3,19},{4,20},{5,21},{6,22},{7,23},{8,24},{9,... | collective-permute-start | bytes 245768 | tf_op jit(solution)/shard_map/ppermute | solution.py:145
  138.7 9.4 %collective-permute-start.5 = (f32[96,256]{1,0:T(8,128)S(1)}, f32[96,256]{1,0:T(8,128)S(1)}, u32[]{:S(2)}, u32[]{:S(2)}) collective-permute-start(f32[96,256]{1,0:T(8,128)S(1)} %pad_maximum_fusion), channel_id=1, source_target_pairs={{0,32},{1,33},{2,34},{3,35},{4,36},{5,37},{6,38},{7,39},{8,40},{9,... | collective-permute-start | bytes 294920 | tf_op jit(solution)/shard_map/ppermute | solution.py:145
  166.8 1.0 copy-start.1
Sparse Core Ops, SparseCore 0:
  10.8 85.7 all-gather.2
where the time goes:
time: 190 us; the launch traced here: 188 us
  waiting for transfers between devices  117 us (62%)
  Pallas kernels  29.7 us (16%)
  between operations  15 us (8%)
  blocking collectives  10.7 us (6%)
  other arithmetic  9.77 us (5%)
  local copies, waits for them, and re-layouts  3.01 us (2%)
  starting transfers between devices  2.65 us (1%)
    all_gather x1, waiting for transfers between devices, local(): group_src = lax.all_gather(src_desc, 'key', axis=0, tiled=True)  85 us
    ppermute x6, waiting for transfers between devices, butterfly(): other = lax.ppermute(jnp.concatenate([lse, weight], axis=0), axis, perm)  31.4 us
    pallas_call x2, Pallas kernels, _sweep(): pl.pallas_call(kernel, out_shape=(out_shape, out_shape), in_specs=[smem,...  29.7 us
    all_gather x1, blocking collectives, local(): all_pack = lax.all_gather(tgt_pack, 'group', axis=0)  10.7 us
    reduce_sum x1, other arithmetic, local(): jnp.sum(group_src.astype(jnp.float32) ** 2, axis=1) / width  5.21 us
  transfers between devices with their start and end apart: 7, of which 7 were waited for; matrix products, arithmetic and copies ran while one was open for 2% of the time, Pallas kernels for 0%

commit v1 on v0

--- a/solution.py
+++ b/solution.py
@@ -21,10 +21,8 @@
     return src_id, tgt_id
 
 
-def _block_cost(src_ref, tgt_ref, sqs_ref, sqt_ref, src_id, tgt_id, width):
-    src_start = pl.multiple_of(src_id * CLUSTER, CLUSTER)
+def _block_cost(src_rows, tgt_ref, sqs_ref, sqt_ref, src_id, tgt_id, width):
     tgt_start = pl.multiple_of(tgt_id * CLUSTER, CLUSTER)
-    src_rows = src_ref[pl.ds(src_start, CLUSTER), :]
     tgt_rows = tgt_ref[pl.ds(tgt_start, CLUSTER), :]
     inner = lax.dot_general(
         tgt_rows, src_rows, (((1,), (1,)), ((), ())), preferred_element_type=jnp.float32
@@ -34,17 +32,57 @@
     return (sq_s + sq_t) - (2.0 / width) * inner
 
 
-def _first_kernel(ids_ref, cnt_ref, src_ref, tgt_ref, sqs_ref, sqt_ref, pot_ref, top_ref, tot_ref):
+def _drive(ids_ref, cnt_ref, src_hbm, src_buf, sems, src_clusters, scores_of, update):
+    count = jnp.minimum(jnp.maximum(cnt_ref[0], 0), ids_ref.shape[1])
+    trips = count // UNROLL
+
+    def copy(slot, buf):
+        src_id = jnp.minimum(jnp.maximum(ids_ref[0, slot], 0), src_clusters - 1)
+        start = pl.multiple_of(src_id * CLUSTER, CLUSTER)
+        return pltpu.make_async_copy(src_hbm.at[pl.ds(start, CLUSTER)], src_buf.at[buf], sems.at[buf])
+
+    @pl.when(trips > 0)
+    def _():
+        for lane in range(UNROLL):
+            copy(lane, lane).start()
+
+    def body(trip, carry):
+        base = (trip % 2) * UNROLL
+        for lane in range(UNROLL):
+            copy(UNROLL * trip + lane, base + lane).wait()
+
+        @pl.when(trip + 1 < trips)
+        def _():
+            ahead = UNROLL - base
+            for lane in range(UNROLL):
+                copy(UNROLL * (trip + 1) + lane, ahead + lane).start()
+
+        blocks = [scores_of(UNROLL * trip + lane, base + lane) for lane in range(UNROLL)]
+        for block in blocks:
+            update(*block)
+        return carry
+
+    def tail(slot, carry):
+        single = copy(slot, 0)
+        single.start()
+        single.wait()
+        update(*scores_of(slot, 0))
+        return carry
+
+    lax.fori_loop(0, trips, body, 0)
+    lax.fori_loop(trips * UNROLL, count, tail, 0)
+
+
+def _first_kernel(ids_ref, cnt_ref, src_hbm, tgt_ref, sqs_ref, sqt_ref, pot_ref, top_ref, tot_ref, src_buf, sems):
     src_clusters = sqs_ref.shape[0]
     tgt_clusters = tgt_ref.shape[0] // CLUSTER
-    width = src_ref.shape[1]
+    width = src_hbm.shape[1]
     top_ref[...] = jnp.full(top_ref.shape, NEG_FLOOR, jnp.float32)
     tot_ref[...] = jnp.zeros(tot_ref.shape, jnp.float32)
-    count = jnp.minimum(jnp.maximum(cnt_ref[0], 0), ids_ref.shape[1])
-
-    def scores_of(slot):
+
+    def scores_of(slot, buf):
         src_id, tgt_id = _slot_ids(ids_ref, slot, src_clusters, tgt_clusters)
-        cost = _block_cost(src_ref, tgt_ref, sqs_ref, sqt_ref, src_id, tgt_id, width)
+        cost = _block_cost(src_buf[buf], tgt_ref, sqs_ref, sqt_ref, src_id, tgt_id, width)
         pot = pot_ref[pl.ds(pl.multiple_of(tgt_id * CLUSTER, CLUSTER), CLUSTER), :]
         return src_id, (pot - cost) * INV_ENTROPY
 
@@ -59,31 +97,19 @@
         top_ref[pl.ds(src_id, 1), :] = new_top
         tot_ref[pl.ds(src_id, 1), :] = new_tot
 
-    def body(trip, carry):
-        blocks = [scores_of(UNROLL * trip + lane) for lane in range(UNROLL)]
-        for block in blocks:
-            update(*block)
-        return carry
-
-    def tail(slot, carry):
-        update(*scores_of(slot))
-        return carry
-
-    lax.fori_loop(0, count // UNROLL, body, 0)
-    lax.fori_loop(count // UNROLL * UNROLL, count, tail, 0)
-
-
-def _second_kernel(ids_ref, cnt_ref, src_ref, tgt_ref, sqs_ref, sqt_ref, dual_ref, top_ref, tot_ref):
+    _drive(ids_ref, cnt_ref, src_hbm, src_buf, sems, src_clusters, scores_of, update)
+
+
+def _second_kernel(ids_ref, cnt_ref, src_hbm, tgt_ref, sqs_ref, sqt_ref, dual_ref, top_ref, tot_ref, src_buf, sems):
     src_clusters = sqs_ref.shape[0]
     tgt_clusters = tgt_ref.shape[0] // CLUSTER
-    width = src_ref.shape[1]
+    width = src_hbm.shape[1]
     top_ref[...] = jnp.full(top_ref.shape, NEG_FLOOR, jnp.float32)
     tot_ref[...] = jnp.zeros(tot_ref.shape, jnp.float32)
-    count = jnp.minimum(jnp.maximum(cnt_ref[0], 0), ids_ref.shape[1])
-
-    def scores_of(slot):
+
+    def scores_of(slot, buf):
         src_id, tgt_id = _slot_ids(ids_ref, slot, src_clusters, tgt_clusters)
-        cost = _block_cost(src_ref, tgt_ref, sqs_ref, sqt_ref, src_id, tgt_id, width)
+        cost = _block_cost(src_buf[buf], tgt_ref, sqs_ref, sqt_ref, src_id, tgt_id, width)
         pot = dual_ref[pl.ds(src_id, 1), :]
         return tgt_id, (pot - cost) * INV_ENTROPY
 
@@ -99,35 +125,30 @@
         top_ref[tgt_rows, :] = new_top
         tot_ref[tgt_rows, :] = new_tot
 
-    def body(trip, carry):
-        blocks = [scores_of(UNROLL * trip + lane) for lane in range(UNROLL)]
-        for block in blocks:
-            update(*block)
-        return carry
-
-    def tail(slot, carry):
-        update(*scores_of(slot))
-        return carry
-
-    lax.fori_loop(0, count // UNROLL, body, 0)
-    lax.fori_loop(count // UNROLL * UNROLL, count, tail, 0)
+    _drive(ids_ref, cnt_ref, src_hbm, src_buf, sems, src_clusters, scores_of, update)
 
 
 def _sweep(kernel, out_shape, ids, cnt, group_src, tgt_desc, sq_src, sq_tgt, pot):
     vmem = pl.BlockSpec(memory_space=pltpu.VMEM)
     smem = pl.BlockSpec(memory_space=pltpu.SMEM)
+    hbm = pl.BlockSpec(memory_space=pl.ANY)
     slots = ids.shape[1]
-    flops = 2 * slots * CLUSTER * CLUSTER * group_src.shape[1]
+    width = group_src.shape[1]
+    flops = 2 * slots * CLUSTER * CLUSTER * width
     return pl.pallas_call(
         kernel,
         out_shape=(out_shape, out_shape),
-        in_specs=[smem, smem, vmem, vmem, vmem, vmem, vmem],
+        in_specs=[smem, smem, hbm, vmem, vmem, vmem, vmem],
         out_specs=(vmem, vmem),
-        compiler_params=pltpu.CompilerParams(vmem_limit_bytes=48 * 1024 * 1024),
+        scratch_shapes=[
+            pltpu.VMEM((2 * UNROLL, CLUSTER, width), group_src.dtype),
+            pltpu.SemaphoreType.DMA((2 * UNROLL,)),
+        ],
+        compiler_params=pltpu.CompilerParams(vmem_limit_bytes=32 * 1024 * 1024),
         cost_estimate=pl.CostEstimate(
             flops=flops,
             transcendentals=slots * CLUSTER * CLUSTER,
-            bytes_accessed=group_src.size * 2 + tgt_desc.size * 2,
+            bytes_accessed=slots * CLUSTER * width * 2 + tgt_desc.size * 2,
         ),
     )(ids, cnt, group_src, tgt_desc, sq_src, sq_tgt, pot)
 

time: 190 us -> 210 us (1.11)
  blocking collectives: 10.7 us -> 27.3 us
  starting transfers between devices: 2.65 us -> 18.4 us
  waiting for transfers between devices: 117 us -> 107 us
  Pallas kernels: 29.7 us -> 21.8 us
  local copies, waits for them, and re-layouts: 3.01 us -> 9.77 us
    all_gather x1, blocking collectives: 10.7 us -> 27.3 us  [local(): all_pack = lax.all_gather(tgt_pack, 'group', axis=0)]
    ppermute x6, starting transfers between devices: 2.61 us -> 18.4 us  [butterfly(): other = lax.ppermute(jnp.concatenate([lse, weight], axis=0), axis, perm)]
    ppermute x6, waiting for transfers between devices: 31.4 us -> 21.1 us  [butterfly(): other = lax.ppermute(jnp.concatenate([lse, weight], axis=0), axis, perm)]
    pallas_call x2, Pallas kernels: 29.7 us -> 21.8 us  [_sweep(): pl.pallas_call(kernel, out_shape=(out_shape, out_shape), in_specs=[smem,...]
    unnamed x11 -> x15, local copies, waits for them, and re-layouts: 0.98 us -> 7.75 us
  transfers between devices with their start and end apart: 7 -> 7, of which waited for: 7 -> 7; matrix products, arithmetic and copies ran while one was open for 2% -> 1% of each run, Pallas kernels for 0% -> 0%
where the time goes in v1:
time: 210 us; the launch traced here: 209 us
  waiting for transfers between devices  107 us (51%)
  blocking collectives  27.3 us (13%)
  Pallas kernels  21.8 us (10%)
  starting transfers between devices  18.4 us (9%)
  between operations  15 us (7%)
  local copies, waits for them, and re-layouts  9.77 us (5%)
  other arithmetic  9.77 us (5%)
    all_gather x1, waiting for transfers between devices, local(): group_src = lax.all_gather(src_desc, 'key', axis=0, tiled=True)  85 us
    all_gather x1, blocking collectives, local(): all_pack = lax.all_gather(tgt_pack, 'group', axis=0)  27.3 us
    pallas_call x2, Pallas kernels, _sweep(): pl.pallas_call(kernel, out_shape=(out_shape, out_shape), in_specs=[smem,...  21.8 us
    ppermute x6, waiting for transfers between devices, butterfly(): other = lax.ppermute(jnp.concatenate([lse, weight], axis=0), axis, perm)  21.1 us
    ppermute x6, starting transfers between devices, butterfly(): other = lax.ppermute(jnp.concatenate([lse, weight], axis=0), axis, perm)  18.4 us
    unnamed x15, local copies, waits for them, and re-layouts  7.75 us
    reduce_sum x1, other arithmetic, local(): jnp.sum(group_src.astype(jnp.float32) ** 2, axis=1) / width  5.21 us
  transfers between devices with their start and end apart: 7, of which 7 were waited for; matrix products, arithmetic and copies ran while one was open for 1% of the time, Pallas kernels for 0%

profile of v1, /device:TPU:8, one launch (start us, length us, event | category | flops | bytes accessed | tf_op | source)
XLA Modules:
  0.0 208.9 jit_solution(15165784099380716557)
XLA Ops:
  7.2 0.0 all-gather.3.cloned.1.call-start
  7.2 0.7 all-gather.3.cloned.1.call-update
  8.6 1.6 multiply_reduce_fusion.1
  10.2 0.4 copy.14.sqt_ref
  10.5 1.1 copy.15.pot_ref
  11.6 0.0 copy-start.6
  11.6 85.0 %all-gather.3.cloned.1.call-done.src_hbm = bf16[16384,256]{1,0:T(8,128)(2,1)} async-done(((bf16[256,256]{1,0:T(8,128)(2,1)}), bf16[16384,256]{1,0:T(8,128)(2,1)}) %all-gather.3.cloned.1.call-update) | async-done | bytes 8388624 | tf_op jit(solution)/shard_map/all_gather | solution.py:186
  96.6 5.2 %multiply_reduce_fusion = f32[16384]{0:T(1024)S(1)} fusion(bf16[16384,256]{1,0:T(8,128)(2,1)} %all-gather.3.cloned.1.call-done.src_hbm), kind=kLoop, calls=%fused_computation | loop fusion | flops 12566528 | bytes 8454144 | tf_op jit(solution)/shard_map/reduce_sum | solution.py:187
  101.9 3.4 %copy-done = bf16[16384,256]{1,0:T(8,128)(2,1)S(1)} copy-done((bf16[16384,256]{1,0:T(8,128)(2,1)S(1)}, bf16[16384,256]{1,0:T(8,128)(2,1)}, u32[]{:S(2)}) %copy-start) | copy-done | bytes 8388632
  105.3 9.5 %shard_map.86 = (f32[64,256]{1,0:T(8,128)S(1)}, f32[64,256]{1,0:T(8,128)S(1)}) custom-call(s32[2,64]{1,0:T(2,128)S(1)} %bitcast.27, s32[1]{0:T(128)} %bitcast.25.cnt_ref, bf16[16384,256]{1,0:T(8,128)(2,1)S(1)} %copy-done, bf16[2048,256]{1,0:T(8,128)(2,1)S(1)} %copy-done.2, f32[64,256]{1,0:T(8,128)S(1)} %div.18.sqs_ref, f32[2048,1]{1,0:T(8,128)S(1)} %copy.14.sqt_ref, ...), custom_call_target="tpu_custom_call" | custom-call | flops 2147483648 | bytes 9437184 | tf_op jit(solution)/shard_map/pallas_call | solution.py:138
  114.8 0.0 copy-start.5
  114.8 8.6 %collective-permute-start = (f32[65,256]{1,0:T(8,128)S(1)}, f32[65,256]{1,0:T(8,128)S(1)}, u32[]{:S(2)}, u32[]{:S(2)}) collective-permute-start(f32[65,256]{1,0:T(8,128)S(1)} %pad_maximum_fusion.2), channel_id=1, source_target_pairs={{0,1},{1,0},{2,3},{3,2},{4,5},{5,4},{6,7},{7,6},{8,9},{9,8},{10,11... | collective-permute-start | bytes 199688 | tf_op jit(solution)/shard_map/ppermute | solution.py:166
  123.4 0.9 collective-permute-done
  124.4 0.1 collective-permute-start.1
  124.5 4.5 %collective-permute-done.1 = f32[66,256]{1,0:T(8,128)S(1)} collective-permute-done((f32[66,256]{1,0:T(8,128)S(1)}, f32[66,256]{1,0:T(8,128)S(1)}, u32[]{:S(2)}, u32[]{:S(2)}) %collective-permute-start.1) | collective-permute-done | bytes 67616 | tf_op jit(solution)/shard_map/ppermute | solution.py:166
  129.1 4.6 %collective-permute-start.2 = (f32[68,256]{1,0:T(8,128)S(1)}, f32[68,256]{1,0:T(8,128)S(1)}, u32[]{:S(2)}, u32[]{:S(2)}) collective-permute-start(f32[68,256]{1,0:T(8,128)S(1)} %pad_maximum_fusion.4), channel_id=1, source_target_pairs={{0,4},{1,5},{2,6},{3,7},{4,0},{5,1},{6,2},{7,3},{8,12},{9,13},{10,... | collective-permute-start | bytes 208904 | tf_op jit(solution)/shard_map/ppermute | solution.py:166
  133.7 2.3 %collective-permute-done.2 = f32[68,256]{1,0:T(8,128)S(1)} collective-permute-done((f32[68,256]{1,0:T(8,128)S(1)}, f32[68,256]{1,0:T(8,128)S(1)}, u32[]{:S(2)}, u32[]{:S(2)}) %collective-permute-start.2) | collective-permute-done | bytes 69664 | tf_op jit(solution)/shard_map/ppermute | solution.py:166
  136.1 1.8 collective-permute-start.3
  137.9 2.7 %collective-permute-done.3 = f32[72,256]{1,0:T(8,128)S(1)} collective-permute-done((f32[72,256]{1,0:T(8,128)S(1)}, f32[72,256]{1,0:T(8,128)S(1)}, u32[]{:S(2)}, u32[]{:S(2)}) %collective-permute-start.3) | collective-permute-done | bytes 73760 | tf_op jit(solution)/shard_map/ppermute | solution.py:166
  140.6 0.2 collective-permute-start.4
  140.8 5.2 %collective-permute-done.4 = f32[80,256]{1,0:T(8,128)S(1)} collective-permute-done((f32[80,256]{1,0:T(8,128)S(1)}, f32[80,256]{1,0:T(8,128)S(1)}, u32[]{:S(2)}, u32[]{:S(2)}) %collective-permute-start.4) | collective-permute-done | bytes 81952 | tf_op jit(solution)/shard_map/ppermute | solution.py:166
  146.1 3.2 %collective-permute-start.5 = (f32[96,256]{1,0:T(8,128)S(1)}, f32[96,256]{1,0:T(8,128)S(1)}, u32[]{:S(2)}, u32[]{:S(2)}) collective-permute-start(f32[96,256]{1,0:T(8,128)S(1)} %pad_maximum_fusion), channel_id=1, source_target_pairs={{0,32},{1,33},{2,34},{3,35},{4,36},{5,37},{6,38},{7,39},{8,40},{9,... | collective-permute-start | bytes 294920 | tf_op jit(solution)/shard_map/ppermute | solution.py:166
  149.3 5.5 %collective-permute-done.5 = f32[96,256]{1,0:T(8,128)S(1)} collective-permute-done((f32[96,256]{1,0:T(8,128)S(1)}, f32[96,256]{1,0:T(8,128)S(1)}, u32[]{:S(2)}, u32[]{:S(2)}) %collective-permute-start.5) | collective-permute-done | bytes 98336 | tf_op jit(solution)/shard_map/ppermute | solution.py:166
  154.8 0.1 fusion.1.dual_ref
  154.8 0.6 constant_dynamic-slice_fusion
  155.4 3.4 %copy-done.1 = bf16[16384,256]{1,0:T(8,128)(2,1)S(1)} copy-done((bf16[16384,256]{1,0:T(8,128)(2,1)S(1)}, bf16[16384,256]{1,0:T(8,128)(2,1)}, u32[]{:S(2)}) %copy-start.1) | copy-done | bytes 8388632
  158.8 12.3 %shard_map.87 = (f32[2048,1]{1,0:T(8,128)S(1)}, f32[2048,1]{1,0:T(8,128)S(1)}) custom-call(s32[2,64]{1,0:T(2,128)S(1)} %bitcast.28, s32[1]{0:T(128)} %bitcast.26.cnt_ref, bf16[16384,256]{1,0:T(8,128)(2,1)S(1)} %copy-done.1, bf16[2048,256]{1,0:T(8,128)(2,1)S(1)} %copy-done.2, f32[64,256]{1,0:T(8,128)S(1)} %div.18.sqs_ref, f32[2048,1]{1,0:T(8,128)S(1)} %copy.14.sqt_ref, ...), custom_call_target="tpu_custom_call" | custom-call | flops 2147483648 | bytes 9437184 | tf_op jit(solution)/shard_map/pallas_call | solution.py:138
  171.1 1.0 copy-done.3
  172.1 1.6 reduce.1
  173.7 0.3 reduce.2
  174.1 27.3 %all-gather = f32[8,8,256]{2,1,0:T(8,128)S(1)} all-gather(f32[2,8,256]{2,1,0:T(8,128)S(1)} %pad_maximum_fusion.8), channel_id=2, replica_groups=mesh['group'=4,'key'=64] {'group'}, dimensions={0}, use_global_device_ids=true | all-gather | bytes 81920 | tf_op jit(solution)/shard_map/all_gather | solution.py:210
  201.5 0.6 multiply_subtract_fusion
  (37 shorter events, 0.5 us)
Async XLA Ops:
  7.2 94.7 %copy-start.2 = (bf16[2048,256]{1,0:T(8,128)(2,1)S(1)}, bf16[2048,256]{1,0:T(8,128)(2,1)}, u32[]{:S(2)}) copy-start(bf16[2048,256]{1,0:T(8,128)(2,1)} %tgt_ref.3) | copy-start | bytes 3145732
  7.2 94.7 %copy-start.4 = (s32[1,1,2,64]{3,2,1,0:T(2,128)S(1)}, s32[1,1,2,64]{3,2,1,0:T(2,128)}, u32[]{:S(2)}) copy-start(s32[1,1,2,64]{3,2,1,0:T(2,128)} %param.12) | copy-start | bytes 1540
  7.2 89.4 %all-gather.3.cloned.1.call-start = ((), (), s32[]{:S(2)}) async-start(), calls=%async_computation | async-start | bytes 8519680 | tf_op jit(solution)/shard_map/all_gather | solution.py:186
  11.6 103.2 %copy-start.6 = (f32[256]{0:T(256)S(1)}, f32[256]{0:T(256)}, u32[]{:S(2)}) copy-start(f32[256]{0:T(256)} %param.9) | copy-start | bytes 3076
  101.9 3.4 %copy-start = (bf16[16384,256]{1,0:T(8,128)(2,1)S(1)}, bf16[16384,256]{1,0:T(8,128)(2,1)}, u32[]{:S(2)}) copy-start(bf16[16384,256]{1,0:T(8,128)(2,1)} %all-gather.3.cloned.1.call-done.src_hbm) | copy-start | bytes 25165828
  114.8 86.7 %copy-start.5 = (f32[2048]{0:T(1024)S(1)}, f32[2048]{0:T(1024)}, u32[]{:S(2)}) copy-start(f32[2048]{0:T(1024)} %param.10) | copy-start | bytes 24580
  114.8 9.5 %collective-permute-start = (f32[65,256]{1,0:T(8,128)S(1)}, f32[65,256]{1,0:T(8,128)S(1)}, u32[]{:S(2)}, u32[]{:S(2)}) collective-permute-start(f32[65,256]{1,0:T(8,128)S(1)} %pad_maximum_fusion.2), channel_id=1, source_target_pairs={{0,1},{1,0},{2,3},{3,2},{4,5},{5,4},{6,7},{7,6},{8,9},{9,8},{10,11... | collective-permute-start | bytes 199688 | tf_op jit(solution)/shard_map/ppermute | solution.py:166
  124.4 4.6 %collective-permute-start.1 = (f32[66,256]{1,0:T(8,128)S(1)}, f32[66,256]{1,0:T(8,128)S(1)}, u32[]{:S(2)}, u32[]{:S(2)}) collective-permute-start(f32[66,256]{1,0:T(8,128)S(1)} %pad_maximum_fusion.3), channel_id=1, source_target_pairs={{0,2},{1,3},{2,0},{3,1},{4,6},{5,7},{6,4},{7,5},{8,10},{9,11},{10,... | collective-permute-start | bytes 202760 | tf_op jit(solution)/shard_map/ppermute | solution.py:166
  129.1 6.9 %collective-permute-start.2 = (f32[68,256]{1,0:T(8,128)S(1)}, f32[68,256]{1,0:T(8,128)S(1)}, u32[]{:S(2)}, u32[]{:S(2)}) collective-permute-start(f32[68,256]{1,0:T(8,128)S(1)} %pad_maximum_fusion.4), channel_id=1, source_target_pairs={{0,4},{1,5},{2,6},{3,7},{4,0},{5,1},{6,2},{7,3},{8,12},{9,13},{10,... | collective-permute-start | bytes 208904 | tf_op jit(solution)/shard_map/ppermute | solution.py:166
  136.1 4.4 %collective-permute-start.3 = (f32[72,256]{1,0:T(8,128)S(1)}, f32[72,256]{1,0:T(8,128)S(1)}, u32[]{:S(2)}, u32[]{:S(2)}) collective-permute-start(f32[72,256]{1,0:T(8,128)S(1)} %pad_maximum_fusion.5), channel_id=1, source_target_pairs={{0,8},{1,9},{2,10},{3,11},{4,12},{5,13},{6,14},{7,15},{8,0},{9,1},... | collective-permute-start | bytes 221192 | tf_op jit(solution)/shard_map/ppermute | solution.py:166
  140.6 5.4 %collective-permute-start.4 = (f32[80,256]{1,0:T(8,128)S(1)}, f32[80,256]{1,0:T(8,128)S(1)}, u32[]{:S(2)}, u32[]{:S(2)}) collective-permute-start(f32[80,256]{1,0:T(8,128)S(1)} %pad_maximum_fusion.1), channel_id=1, source_target_pairs={{0,16},{1,17},{2,18},{3,19},{4,20},{5,21},{6,22},{7,23},{8,24},{9,... | collective-permute-start | bytes 245768 | tf_op jit(solution)/shard_map/ppermute | solution.py:166
  146.1 8.6 %collective-permute-start.5 = (f32[96,256]{1,0:T(8,128)S(1)}, f32[96,256]{1,0:T(8,128)S(1)}, u32[]{:S(2)}, u32[]{:S(2)}) collective-permute-start(f32[96,256]{1,0:T(8,128)S(1)} %pad_maximum_fusion), channel_id=1, source_target_pairs={{0,32},{1,33},{2,34},{3,35},{4,36},{5,37},{6,38},{7,39},{8,40},{9,... | collective-permute-start | bytes 294920 | tf_op jit(solution)/shard_map/ppermute | solution.py:166
  155.4 3.4 %copy-start.1 = (bf16[16384,256]{1,0:T(8,128)(2,1)S(1)}, bf16[16384,256]{1,0:T(8,128)(2,1)}, u32[]{:S(2)}) copy-start(bf16[16384,256]{1,0:T(8,128)(2,1)} %all-gather.3.cloned.1.call-done.src_hbm) | copy-start | bytes 25165828
  171.1 1.0 copy-start.3
Sparse Core Ops, SparseCore 0:
  10.8 85.7 all-gather.2
